TPU v7x, 32 devices: a whole 2x2x4 slice. The times are simulated.
32 devices in a mesh: layer: 2 (over x), row: 4 (over y, core), col: 4 (over z).
Axes of the slice: x: 2, y: 2, z: 4, core: 2. Of those that a mesh axis runs over, the one named last changes fastest.
Arguments:
- left_matrix: bfloat16 [8192, 1024], P('row', ('layer', 'col')), may hold values from -6 to 6
- square_term: bfloat16 [1024, 1024], P(('layer', 'row'), 'col'), may hold values from -0.5 to 0.5
- block_pattern: int32 [64, 8], replicated, may hold values from 0 to 1, as said below
- keep_mask: int32 [64, 8], replicated, may hold values 0 or 1
Outputs:
- product: bfloat16 [8192, 1024], P('row', 'col')
Inputs may be any that keep to these rules, and one draw needn't show every extreme that they name: `block_pattern`: in each aligned group of 16 block rows, every block column holds 1 to 8 stored blocks; some group holds exactly 8.
All inputs are finite; a program needn't handle non-finite values.
Results may differ from a plain program's by a relative error of at most 0.0038.
Values may be sent and summed in bfloat16 or wider, within the bound.
No kernel may reach another device: no remote copies, remote signals or barrier semaphores. Data moves between devices by JAX's collectives and lax.ppermute only.
A program may use at most 64 MiB of HBM per device.

v0:
```python
import jax
import jax.numpy as jnp
from jax import lax
from jax.sharding import PartitionSpec as P

BLK = 128


def expand(mask_blocks):
    return jnp.repeat(jnp.repeat(mask_blocks, BLK, axis=0), BLK, axis=1)


def per_device(left_matrix, square_term, block_pattern, keep_mask):
    row_idx = lax.axis_index("row")
    col_idx = lax.axis_index("col")
    layer_idx = lax.axis_index("layer")
    row_count = lax.axis_size("row")
    col_count = lax.axis_size("col")
    rows_local = left_matrix.shape[0]
    row_blocks = rows_local // BLK
    inner_blocks = left_matrix.shape[1] // BLK
    inner_local = square_term.shape[0]
    cols_local = square_term.shape[1]
    col_blocks = cols_local // BLK
    inner_start = (layer_idx * col_count + col_idx) * inner_blocks
    pattern_patch = lax.dynamic_slice(
        block_pattern, (row_idx * row_blocks, inner_start), (row_blocks, inner_blocks)
    )
    first_inner = (layer_idx * row_count + row_idx) * inner_local
    first_col = col_idx * cols_local
    inner_pos = first_inner + lax.broadcasted_iota(jnp.int32, (inner_local, cols_local), 0)
    col_pos = first_col + lax.broadcasted_iota(jnp.int32, (inner_local, cols_local), 1)
    unit = jnp.where(inner_pos == col_pos, jnp.float32(1.5), jnp.float32(0.0))
    right_factor = (unit - 0.5 * square_term.astype(jnp.float32)).astype(jnp.bfloat16)
    right_half = lax.all_gather(right_factor, "row", axis=0, tiled=True)
    sparse_left = jnp.where(expand(pattern_patch) > 0, left_matrix, jnp.zeros_like(left_matrix))
    partial_sum = jnp.dot(
        lax.all_gather(sparse_left, "col", axis=1, tiled=True),
        right_half,
        preferred_element_type=jnp.float32,
    )
    keep_patch = lax.dynamic_slice(
        keep_mask, (row_idx * row_blocks, col_idx * col_blocks), (row_blocks, col_blocks)
    )
    keep_full = expand(keep_patch)
    full_sum = lax.psum(partial_sum, "layer")
    kept = jnp.where(keep_full > 0, full_sum, jnp.zeros_like(full_sum))
    return kept.astype(jnp.bfloat16)


def solution(mesh):
    return jax.shard_map(
        per_device,
        mesh=mesh,
        in_specs=(P("row", ("layer", "col")), P(("layer", "row"), "col"), P(), P()),
        out_specs=P("row", "col"),
        check_vma=False,
    )
```

profile of v0, /device:TPU:0, one launch (start us, length us, event | category | flops | bytes accessed | tf_op | source)
XLA Modules:
  0.0 123.4 jit_solution(1267802918335464349)
XLA Ops:
  6.5 0.0 copy-start
  6.5 0.0 all-gather.2.cloned.1.call-start
  6.5 0.8 compare_bitcast_fusion
  7.3 0.1 broadcast_bitcast_fusion.1
  7.4 2.2 %broadcast_select_fusion = bf16[2048,128]{1,0:T(8,128)(2,1)} fusion(bf16[2048,128]{1,0:T(8,128)(2,1)} %param.4, pred[2048]{0:T(1024)(128)(4,1)S(1)} %broadcast_bitcast_fusion.1), kind=kLoop, calls=%fused_computation.1 | loop fusion | flops 262144 | bytes 1050624 | tf_op jit(solution)/shard_map/jit(_where)/select_n | solution.py:36
  9.6 0.0 all-gather.2.cloned.1.call-update
  9.6 0.8 dynamic-slice_compare_fusion
  10.4 0.1 broadcast_bitcast_fusion
  10.5 0.2 broadcast_in_dim.25
  10.7 1.5 %copy.6 = pred[2048,256]{1,0:T(8,128)(4,1)} copy(pred[2048,256]{0,1:T(8,128)(4,1)S(1)} %bitcast.14) | data formatting | bytes 1048576 | tf_op jit(solution)/shard_map/gt | solution.py:47
  12.2 0.0 copy-done
  12.2 0.1 subtract_convert_fusion
  12.3 7.2 %all_gather.7 = bf16[512,256]{1,0:T(8,128)(2,1)S(1)} all-gather(bf16[128,256]{1,0:T(8,128)(2,1)S(1)} %subtract_convert_fusion), channel_id=1, replica_groups=mesh['layer'=2,'row'=4,'col'=4] {'row'}, dimensions={0}, use_global_device_ids=true | all-gather | bytes 327680 | tf_op jit(solution)/shard_map/all_gather | solution.py:35
  19.5 39.2 %all-gather.2.cloned.1.call-done = bf16[2048,512]{1,0:T(8,128)(2,1)} async-done(((bf16[2048,128]{1,0:T(8,128)(2,1)}), bf16[2048,512]{1,0:T(8,128)(2,1)}) %all-gather.2.cloned.1.call-update) | async-done | bytes 2097168 | tf_op jit(solution)/shard_map/all_gather | solution.py:38
  58.7 2.3 %fusion = f32[2048,256]{1,0:T(8,128)S(1)} fusion(bf16[2048,512]{1,0:T(8,128)(2,1)} %all-gather.2.cloned.1.call-done, bf16[512,256]{1,0:T(8,128)(2,1)S(1)} %all_gather.7), kind=kOutput, calls=%fused_computation.10 | convolution fusion | flops 536870912 | bytes 4456448 | tf_op jit(solution)/shard_map/dot_general | solution.py:37
  61.0 53.2 %all-reduce.1 = bf16[2048,256]{1,0:T(8,128)(2,1)S(1)} all-reduce(f32[2048,256]{1,0:T(8,128)S(1)} %fusion), channel_id=1, replica_groups=mesh['layer'=2,'row'=4,'col'=4] {'layer'}, use_global_device_ids=true, to_apply=%region_0.1 | all-reduce | flops 524288 | bytes 3145728 | tf_op jit(solution)/shard_map/psum | solution.py:46
  114.2 2.3 %select_convert_fusion = bf16[2048,256]{1,0:T(8,128)(2,1)} fusion(pred[2048,256]{1,0:T(8,128)(4,1)} %copy.6, bf16[2048,256]{1,0:T(8,128)(2,1)S(1)} %all-reduce.1), kind=kLoop, calls=%fused_computation | loop fusion | flops 524288 | bytes 2621440 | tf_op jit(solution)/shard_map/convert_element_type | solution.py:48
  (3 shorter events, 0.0 us)
Async XLA Ops:
  6.5 5.6 %copy-start = (bf16[128,256]{1,0:T(8,128)(2,1)S(1)}, bf16[128,256]{1,0:T(8,128)(2,1)}, u32[]{:S(2)}) copy-start(bf16[128,256]{1,0:T(8,128)(2,1)} %param.5) | copy-start | bytes 196612
  6.5 52.2 %all-gather.2.cloned.1.call-start = ((), (), s32[]{:S(2)}) async-start(), calls=%async_computation | async-start | bytes 2621440 | tf_op jit(solution)/shard_map/all_gather | solution.py:38
Sparse Core Ops, SparseCore 0:
  9.7 48.9 all-gather.1
where the time goes:
time: 124 us; the launch traced here: 123 us
  blocking collectives  60.4 us (49%)
  waiting for transfers between devices  39.2 us (32%)
  between operations  13.4 us (11%)
  other arithmetic  6.15 us (5%)
  matrix products  2.29 us (2%)
  local copies, waits for them, and re-layouts  1.83 us (1%)
    psum x1, blocking collectives, per_device(): full_sum = lax.psum(partial_sum, 'layer')  53.2 us
    all_gather x1, waiting for transfers between devices, per_device(): lax.all_gather(sparse_left, 'col', axis=1, tiled=True)  39.2 us
    all_gather x1, blocking collectives, per_device(): right_half = lax.all_gather(right_factor, 'row', axis=0, tiled=True)  7.22 us
  transfers between devices with their start and end apart: 1, of which 1 were waited for; matrix products, arithmetic and copies ran while one was open for 2% of the time, Pallas kernels for 0%

commit v1 on v0

--- a/solution.py
+++ b/solution.py
@@ -32,7 +32,12 @@
     col_pos = first_col + lax.broadcasted_iota(jnp.int32, (inner_local, cols_local), 1)
     unit = jnp.where(inner_pos == col_pos, jnp.float32(1.5), jnp.float32(0.0))
     right_factor = (unit - 0.5 * square_term.astype(jnp.float32)).astype(jnp.bfloat16)
-    right_half = lax.all_gather(right_factor, "row", axis=0, tiled=True)
+    ring = [right_factor]
+    for hop in range(3):
+        ring.append(lax.ppermute(ring[-1], "row", [(dev, (dev + 1) % 4) for dev in range(4)]))
+    right_half = jnp.roll(
+        jnp.concatenate(ring[::-1], axis=0), (lax.axis_index("row") + 1) * ring[0].shape[0], axis=0
+    )
     sparse_left = jnp.where(expand(pattern_patch) > 0, left_matrix, jnp.zeros_like(left_matrix))
     partial_sum = jnp.dot(
         lax.all_gather(sparse_left, "col", axis=1, tiled=True),

time: 124 us -> 124 us (level)
  blocking collectives: 60.4 us -> 53.2 us
  waiting for transfers between devices: 39.2 us -> 44.8 us
    ppermute x0 -> x3, waiting for transfers between devices: none -> 8.66 us  [per_device(): lax.ppermute(ring[-1], 'row', [(dev, (dev + 1) % 4) for dev in range(4)])]
    all_gather x1 -> x0, blocking collectives: 7.22 us -> none  [per_device(): right_half = lax.all_gather(right_factor, 'row', axis=0, tiled=True)]
    all_gather x1, waiting for transfers between devices: 39.2 us -> 36.1 us  [per_device(): lax.all_gather(sparse_left, 'col', axis=1, tiled=True)]
  transfers between devices with their start and end apart: 1 -> 4, of which waited for: 1 -> 4; matrix products, arithmetic and copies ran while one was open for 2% -> 3% of each run, Pallas kernels for 0% -> 0%
where the time goes in v1:
time: 124 us; the launch traced here: 123 us
  blocking collectives  53.2 us (43%)
  waiting for transfers between devices  44.8 us (36%)
  between operations  13.5 us (11%)
  other arithmetic  7.16 us (6%)
  matrix products  2.3 us (2%)
  local copies, waits for them, and re-layouts  1.85 us (1%)
    psum x1, blocking collectives, per_device(): full_sum = lax.psum(partial_sum, 'layer')  53.2 us
    all_gather x1, waiting for transfers between devices, per_device(): lax.all_gather(sparse_left, 'col', axis=1, tiled=True)  36.1 us
    ppermute x3, waiting for transfers between devices, per_device(): lax.ppermute(ring[-1], 'row', [(dev, (dev + 1) % 4) for dev in range(4)])  8.66 us
  transfers between devices with their start and end apart: 4, of which 4 were waited for; matrix products, arithmetic and copies ran while one was open for 3% of the time, Pallas kernels for 0%

profile of v1, /device:TPU:0, one launch (start us, length us, event | category | flops | bytes accessed | tf_op | source)
XLA Modules:
  0.0 123.4 jit_solution(15491808068265470410)
XLA Ops:
  6.5 0.0 copy-start
  6.5 0.0 all-gather.2.cloned.1.call-start
  6.5 0.8 compare_bitcast_fusion
  7.3 0.1 broadcast_bitcast_fusion.1
  7.4 2.2 %broadcast_select_fusion = bf16[2048,128]{1,0:T(8,128)(2,1)} fusion(bf16[2048,128]{1,0:T(8,128)(2,1)} %param.4, pred[2048]{0:T(1024)(128)(4,1)S(1)} %broadcast_bitcast_fusion.1), kind=kLoop, calls=%fused_computation.1 | loop fusion | flops 262144 | bytes 1050624 | tf_op jit(solution)/shard_map/jit(_where)/select_n | solution.py:41
  9.6 0.0 all-gather.2.cloned.1.call-update
  9.6 0.9 subtract_convert_fusion
  10.6 0.5 collective-permute-start
  11.1 3.9 %collective-permute-done = bf16[128,256]{1,0:T(8,128)(2,1)S(1)} collective-permute-done((bf16[128,256]{1,0:T(8,128)(2,1)S(1)}, bf16[128,256]{1,0:T(8,128)(2,1)S(1)}, u32[]{:S(2)}, u32[]{:S(2)}) %collective-permute-start) | collective-permute-done | bytes 65568 | tf_op jit(solution)/shard_map/ppermute | solution.py:37
  15.0 0.1 collective-permute-start.1
  15.0 0.8 dynamic-slice_compare_fusion
  15.8 2.9 %collective-permute-done.1 = bf16[128,256]{1,0:T(8,128)(2,1)S(1)} collective-permute-done((bf16[128,256]{1,0:T(8,128)(2,1)S(1)}, bf16[128,256]{1,0:T(8,128)(2,1)S(1)}, u32[]{:S(2)}, u32[]{:S(2)}) %collective-permute-start.1) | collective-permute-done | bytes 65568 | tf_op jit(solution)/shard_map/ppermute | solution.py:37
  18.7 0.1 collective-permute-start.2
  18.7 0.1 broadcast_bitcast_fusion
  18.8 0.2 broadcast_in_dim.25
  19.0 1.4 %copy.6 = pred[2048,256]{1,0:T(8,128)(4,1)} copy(pred[2048,256]{0,1:T(8,128)(4,1)S(1)} %bitcast.13) | data formatting | bytes 1048576 | tf_op jit(solution)/shard_map/gt | solution.py:52
  20.5 1.9 %collective-permute-done.2 = bf16[128,256]{1,0:T(8,128)(2,1)S(1)} collective-permute-done((bf16[128,256]{1,0:T(8,128)(2,1)S(1)}, bf16[128,256]{1,0:T(8,128)(2,1)S(1)}, u32[]{:S(2)}, u32[]{:S(2)}) %collective-permute-start.2) | collective-permute-done | bytes 65568 | tf_op jit(solution)/shard_map/ppermute | solution.py:37
  22.4 0.0 copy-done
  22.4 0.1 constant_dynamic-update-slice_fusion.4
  22.5 0.1 constant_dynamic-update-slice_fusion
  22.6 36.1 %all-gather.2.cloned.1.call-done = bf16[2048,512]{1,0:T(8,128)(2,1)} async-done(((bf16[2048,128]{1,0:T(8,128)(2,1)}), bf16[2048,512]{1,0:T(8,128)(2,1)}) %all-gather.2.cloned.1.call-update) | async-done | bytes 2097168 | tf_op jit(solution)/shard_map/all_gather | solution.py:43
  58.8 2.3 %fusion = f32[2048,256]{1,0:T(8,128)S(1)} fusion(bf16[2048,512]{1,0:T(8,128)(2,1)} %all-gather.2.cloned.1.call-done, bf16[1024,256]{1,0:T(8,128)(2,1)S(1)} %constant_dynamic-update-slice_fusion, s32[]{:T(128)S(6)} %select_n.41), kind=kOutput, calls=%fused_computation.2 | convolution fusion | flops 536870912 | bytes 4456452 | tf_op jit(solution)/shard_map/dot_general | solution.py:42
  61.1 53.2 %all-reduce.1 = bf16[2048,256]{1,0:T(8,128)(2,1)S(1)} all-reduce(f32[2048,256]{1,0:T(8,128)S(1)} %fusion), channel_id=1, replica_groups=mesh['layer'=2,'row'=4,'col'=4] {'layer'}, use_global_device_ids=true, to_apply=%region_0.1 | all-reduce | flops 524288 | bytes 3145728 | tf_op jit(solution)/shard_map/psum | solution.py:51
  114.2 2.3 %select_convert_fusion = bf16[2048,256]{1,0:T(8,128)(2,1)} fusion(pred[2048,256]{1,0:T(8,128)(4,1)} %copy.6, bf16[2048,256]{1,0:T(8,128)(2,1)S(1)} %all-reduce.1), kind=kLoop, calls=%fused_computation | loop fusion | flops 524288 | bytes 2621440 | tf_op jit(solution)/shard_map/convert_element_type | solution.py:53
  (9 shorter events, 0.1 us)
Async XLA Ops:
  6.5 15.9 %copy-start = (bf16[128,256]{1,0:T(8,128)(2,1)S(1)}, bf16[128,256]{1,0:T(8,128)(2,1)}, u32[]{:S(2)}) copy-start(bf16[128,256]{1,0:T(8,128)(2,1)} %param.5) | copy-start | bytes 196612
  6.5 52.2 %all-gather.2.cloned.1.call-start = ((), (), s32[]{:S(2)}) async-start(), calls=%async_computation | async-start | bytes 2621440 | tf_op jit(solution)/shard_map/all_gather | solution.py:43
  10.6 4.4 %collective-permute-start = (bf16[128,256]{1,0:T(8,128)(2,1)S(1)}, bf16[128,256]{1,0:T(8,128)(2,1)S(1)}, u32[]{:S(2)}, u32[]{:S(2)}) collective-permute-start(bf16[128,256]{1,0:T(8,128)(2,1)S(1)} %subtract_convert_fusion), channel_id=1, source_target_pairs={{0,4},{4,8},{8,12},{12,0},{1,5},{5,9},{9,13},{13,1},{2,6},{6,10},{... | collective-permute-start | bytes 196616 | tf_op jit(solution)/shard_map/ppermute | solution.py:37
  15.0 3.7 %collective-permute-start.1 = (bf16[128,256]{1,0:T(8,128)(2,1)S(1)}, bf16[128,256]{1,0:T(8,128)(2,1)S(1)}, u32[]{:S(2)}, u32[]{:S(2)}) collective-permute-start(bf16[128,256]{1,0:T(8,128)(2,1)S(1)} %collective-permute-done), channel_id=1, source_target_pairs={{0,4},{4,8},{8,12},{12,0},{1,5},{5,9},{9,13},{13,1},{2,6},{6,10},{... | collective-permute-start | bytes 196616 | tf_op jit(solution)/shard_map/ppermute | solution.py:37
  18.7 3.7 %collective-permute-start.2 = (bf16[128,256]{1,0:T(8,128)(2,1)S(1)}, bf16[128,256]{1,0:T(8,128)(2,1)S(1)}, u32[]{:S(2)}, u32[]{:S(2)}) collective-permute-start(bf16[128,256]{1,0:T(8,128)(2,1)S(1)} %collective-permute-done.1), channel_id=1, source_target_pairs={{0,4},{4,8},{8,12},{12,0},{1,5},{5,9},{9,13},{13,1},{2,6},{6,10},{... | collective-permute-start | bytes 196616 | tf_op jit(solution)/shard_map/ppermute | solution.py:37
Sparse Core Ops, SparseCore 0:
  9.7 48.9 all-gather.1
